TPU v7x, 32 devices: a whole 2x2x4 slice. The times are simulated.
32 devices in a mesh: space: 8 (over z, y), chan: 4 (over x, core).
Axes of the slice: x: 2, y: 2, z: 4, core: 2. Of those that a mesh axis runs over, the one named last changes fastest.
Arguments:
- positions: float32 [3, 2048], P(None, 'space'), may hold values from 0 to 2
- features: bfloat16 [128, 2048], P('chan', 'space'), may hold values from -6 to 6
- send_rows: int32 [24, 128], P('space'), may hold values from 0 to 255, as said below
- pair_tiles: int32 [64, 2], P('space'), may hold values from 0 to 4, as said below
- tile_live: int32 [64], P('space'), may hold values from 0 to 1, as said below
- radial_weight: float32 [128, 8], P('chan'), may hold values from -1 to 1
- mix_weight: bfloat16 [3, 128, 128], replicated, may hold values from -0.5 to 0.5
- out_grad: bfloat16 [128, 9, 2048], P('chan', None, 'space'), may hold values from -6 to 6
Outputs:
- output: bfloat16 [128, 9, 2048], P('chan', None, 'space')
- grad_features: bfloat16 [128, 2048], P('chan', 'space')
- forces: float32 [3, 2048], P(None, 'space')
- grad_radial: float32 [128, 8], P('chan')
Inputs may be any that keep to these rules, and one draw needn't show every extreme that they name: `send_rows`: row s * 3 + b lists 128 distinct atoms of domain s, numbered within the domain, that domain s sends to domain s xor 2^b. `pair_tiles`: row s * 8 + t holds domain s's tile t: a target block below 2 among its own blocks, then a source block below 5 among its source blocks. `tile_live`: on each domain the live tiles come first; each domain has 2 or more live tiles, and some domain has all 8.
All inputs are finite; a program needn't handle non-finite values.
Results may differ from a plain program's by a relative error of at most 0.025.
Values may be sent and summed in bfloat16 or wider, within the bound.
No kernel may reach another device: no remote copies, remote signals or barrier semaphores. Data moves between devices by JAX's collectives and lax.ppermute only.
A program may use at most 64 MiB of HBM per device.

v0:
```python
import math
import jax
import jax.numpy as jnp
from jax import lax
from jax.sharding import PartitionSpec as P

SOFTENING = 0.25
CUTOFF = 2.5
CUTOFF_SQ = 6.25
SHARPNESS = 10.0
ROOT_THREE = math.sqrt(3.0)
ORDER_OF = (0, 1, 1, 1, 2, 2, 2, 2, 2)


def partner(value, axis, bit):
    mask = 2**bit
    pairs = [(source, source ^ mask) for source in range(lax.axis_size(axis))]
    return lax.ppermute(value, axis, pairs)


def geometry(target_pos, source_pos, pair_keep, radial_count):
    offset = source_pos[:, None, :] - target_pos[:, :, None]
    dist_sq = jnp.sum(offset * offset, axis=0) + SOFTENING
    distance = jnp.sqrt(dist_sq)
    along_x = offset[0] / distance
    along_y = offset[1] / distance
    along_z = offset[2] / distance
    harmonics = jnp.stack(
        [
            jnp.ones_like(along_x),
            along_x,
            along_y,
            along_z,
            ROOT_THREE * along_x * along_y,
            ROOT_THREE * along_y * along_z,
            ROOT_THREE * along_x * along_z,
            0.5 * (3.0 * along_z * along_z - 1.0),
            0.5 * ROOT_THREE * (along_x * along_x - along_y * along_y),
        ]
    )
    envelope = jnp.square(jnp.maximum(1.0 - dist_sq / CUTOFF_SQ, 0.0)) * pair_keep
    centers = (jnp.arange(radial_count, dtype=jnp.float32) + 0.5) * (CUTOFF / radial_count)
    radial = (
        jnp.exp(-SHARPNESS * jnp.square(distance[None] - centers[:, None, None])) * envelope[None]
    )
    return (harmonics, radial)


def take_block(array, blk_index, block_size):
    return lax.dynamic_slice_in_dim(array, blk_index * block_size, block_size, array.ndim - 1)


def add_block(array, blk_index, value, block_size):
    current = take_block(array, blk_index, block_size)
    return lax.dynamic_update_slice_in_dim(
        array, current + value, blk_index * block_size, array.ndim - 1
    )


def body(
    positions, features, send_rows, pair_tiles, tile_live, radial_weight, mix_weight, out_grad
):
    block_size = send_rows.shape[1]
    atoms_dev = positions.shape[1]
    chan_dev = features.shape[0]
    radial_count = radial_weight.shape[1]
    components = out_grad.shape[1]
    levels = lax.axis_size("space").bit_length() - 1
    pos_list = [positions]
    feat_list = [features]
    for level_bit in range(levels):
        sent_rows = send_rows[level_bit]
        got_feat, got_pos = (
            partner(
                jnp.take(features, sent_rows, axis=1).astype(jnp.float32), "space", level_bit
            ).astype(jnp.bfloat16),
            partner(jnp.take(positions, sent_rows, axis=1), "space", level_bit),
        )
        feat_list.append(got_feat)
        pos_list.append(got_pos)
    src_pos = jnp.concatenate(pos_list, axis=1)
    src_feat = jnp.concatenate(feat_list, axis=1)
    src_atoms = src_pos.shape[1]
    live_count = jnp.sum(tile_live)

    def tile_parts(tile_index):
        target_blk = pair_tiles[tile_index, 0]
        source_blk = pair_tiles[tile_index, 1]
        same = (target_blk == source_blk).astype(jnp.float32)
        pair_keep = 1.0 - same * jnp.eye(block_size, dtype=jnp.float32)
        target_pos = take_block(src_pos, target_blk, block_size)
        source_pos = take_block(src_pos, source_blk, block_size)

        def geo_fn(first_pos, second_pos):
            return geometry(first_pos, second_pos, pair_keep, radial_count)

        return (target_blk, source_blk, target_pos, source_pos, geo_fn)

    def forward_tile(tile_index, moments):
        target_blk, source_blk, target_pos, source_pos, geo_fn = tile_parts(tile_index)
        harmonics, radial = geo_fn(target_pos, source_pos)
        source_feat = take_block(src_feat, source_blk, block_size)
        pieces_list = []
        for harmonic in range(components):
            pair_values = (harmonics[harmonic][None] * radial).astype(jnp.bfloat16)
            message = jnp.einsum(
                "kij,cj->cki", pair_values, source_feat, preferred_element_type=jnp.float32
            )
            pieces_list.append(jnp.einsum("cki,ck->ci", message, radial_weight))
        contrib = jnp.stack(pieces_list, axis=1)
        return add_block(moments, target_blk, contrib, block_size)

    moments = lax.fori_loop(
        0, live_count, forward_tile, jnp.zeros((chan_dev, components, atoms_dev), jnp.float32)
    )
    packed = moments.astype(jnp.bfloat16)
    mixing = jnp.take(mix_weight, jnp.array(ORDER_OF, dtype=jnp.int32), axis=0)
    offset = lax.axis_index("chan") * chan_dev
    gathered_piece = lax.all_gather(packed, "chan", axis=0, tiled=True)
    weight_part = lax.dynamic_slice(
        mixing, (0, offset, 0), (components, chan_dev, gathered_piece.shape[0])
    )
    mixed_out = jnp.einsum(
        "lxc,cli->xli", weight_part, gathered_piece, preferred_element_type=jnp.float32
    )
    scalar_part = mixed_out[:, 0, :]
    gate_value = jax.nn.sigmoid(scalar_part)
    result = jnp.concatenate(
        [(scalar_part * gate_value)[:, None, :], mixed_out[:, 1:, :] * gate_value[:, None, :]],
        axis=1,
    ).astype(jnp.bfloat16)
    upstream = out_grad.astype(jnp.float32)
    scalar_grad = upstream[:, 0, :] * (
        gate_value * (1.0 + scalar_part * (1.0 - gate_value))
    ) + gate_value * (1.0 - gate_value) * jnp.sum(upstream[:, 1:, :] * mixed_out[:, 1:, :], axis=1)
    rest_grad = upstream[:, 1:, :] * gate_value[:, None, :]
    dz_packed = jnp.concatenate([scalar_grad[:, None, :], rest_grad], axis=1).astype(jnp.bfloat16)
    gathered_piece = lax.all_gather(dz_packed, "chan", axis=0, tiled=True)
    weight_part = lax.dynamic_slice(
        mixing, (0, 0, offset), (components, gathered_piece.shape[0], chan_dev)
    )
    moment_grad_all = jnp.einsum(
        "lxc,xli->cli", weight_part, gathered_piece, preferred_element_type=jnp.float32
    )

    def backward_tile(tile_index, running):
        grad_src, dpos_src, grad_rad = running
        target_blk, source_blk, target_pos, source_pos, geo_fn = tile_parts(tile_index)
        (harmonics, radial), pullback = jax.vjp(geo_fn, target_pos, source_pos)
        source_feat = take_block(src_feat, source_blk, block_size)
        moment_grad = take_block(moment_grad_all, target_blk, block_size)
        grad_source = jnp.zeros((chan_dev, block_size), jnp.float32)
        rad_grad = jnp.zeros_like(radial)
        harm_list = []
        for harmonic in range(components):
            pair_values = (harmonics[harmonic][None] * radial).astype(jnp.bfloat16)
            message = jnp.einsum(
                "kij,cj->cki", pair_values, source_feat, preferred_element_type=jnp.float32
            )
            grad_rad = grad_rad + jnp.einsum("cki,ci->ck", message, moment_grad[:, harmonic, :])
            weighted = (radial_weight[:, :, None] * moment_grad[:, harmonic, None, :]).astype(
                jnp.bfloat16
            )
            grad_source = grad_source + jnp.einsum(
                "cki,kij->cj", weighted, pair_values, preferred_element_type=jnp.float32
            )
            value_grad = jnp.einsum(
                "cki,cj->kij", weighted, source_feat, preferred_element_type=jnp.float32
            )
            harm_list.append(jnp.sum(value_grad * radial, axis=0))
            rad_grad = rad_grad + value_grad * harmonics[harmonic][None]
        target_grad, source_grad_pos = pullback((jnp.stack(harm_list), rad_grad))
        grad_src = add_block(grad_src, source_blk, grad_source, block_size)
        dpos_src = add_block(dpos_src, target_blk, target_grad, block_size)
        dpos_src = add_block(dpos_src, source_blk, source_grad_pos, block_size)
        return (grad_src, dpos_src, grad_rad)

    init = (
        jnp.zeros((chan_dev, src_atoms), jnp.float32),
        jnp.zeros((3, src_atoms), jnp.float32),
        jnp.zeros((chan_dev, radial_count), jnp.float32),
    )
    grad_src, dpos_src, grad_rad = lax.fori_loop(0, live_count, backward_tile, init)
    dpos_src = lax.psum(dpos_src, "chan")
    own_grad = grad_src[:, :atoms_dev]
    own_dpos = dpos_src[:, :atoms_dev]
    for level_bit in range(levels):
        low = atoms_dev + level_bit * block_size
        back_grad, back_pos = partner(
            (grad_src[:, low : low + block_size], dpos_src[:, low : low + block_size]),
            "space",
            level_bit,
        )
        sent_rows = send_rows[level_bit]
        own_grad = own_grad.at[:, sent_rows].add(back_grad)
        own_dpos = own_dpos.at[:, sent_rows].add(back_pos)
    grad_radial = lax.psum(grad_rad, "space")
    return (result, own_grad.astype(jnp.bfloat16), -own_dpos, grad_radial)


def solution(mesh):
    placed = (
        P(None, "space"),
        P("chan", "space"),
        P("space", None),
        P("space", None),
        P("space"),
        P("chan", None),
        P(),
        P("chan", None, "space"),
    )
    return jax.shard_map(
        body,
        mesh=mesh,
        in_specs=placed,
        out_specs=(P("chan", None, "space"), P("chan", "space"), P(None, "space"), P("chan", None)),
        check_vma=False,
    )
```

profile of v0, /device:TPU:0, one launch (start us, length us, event | category | flops | bytes accessed | tf_op | source)
XLA Modules:
  0.0 354.6 jit_solution(2762358216147547025)
XLA Ops:
  2.4 4.1 %collective-permute-start.2 = (bf16[32,128]{1,0:T(8,128)(2,1)S(1)}, bf16[32,128]{1,0:T(8,128)(2,1)S(1)}, u32[]{:S(2)}, u32[]{:S(2)}) collective-permute-start(bf16[32,128]{1,0:T(8,128)(2,1)S(1)} %bitcast_convert_fusion), channel_id=1, source_target_pairs={{0,16},{4,20},{8,24},{12,28},{16,0},{20,4},{24,8},{28,12},{1,17},{... | collective-permute-start | bytes 24584 | tf_op jit(solution)/shard_map/ppermute | solution.py:18
  7.3 1.6 collective-permute-start.1
  12.4 1.6 collective-permute-start.3
  18.2 2.9 collective-permute-done
  21.8 19.3 %while.28 = (s32[]{:T(128)}, f32[32,9,256]{2,0,1:T(8,128)S(1)}, s32[]{:T(128)}, s32[8,2]{0,1:T(2,128)S(1)}, bf16[32,640]{1,0:T(8,128)(2,1)S(1)}, /*index=5*/f32[...) while((s32[]{:T(128)}, f32[32,9,256]{2,0,1:T(8,128)S(1)}, ...), condition=%wide.region_3.6_spmd, body=%wide.region_1.5_spmd.sunk | while | flops 83677216 | bytes 5811606 | solution.py:113
  41.7 7.5 %all_gather.6 = bf16[128,9,256]{2,0,1:T(8,128)(2,1)S(1)} all-gather(bf16[32,9,256]{2,0,1:T(8,128)(2,1)S(1)} %convert_element_type.217), channel_id=1, replica_groups=mesh['space'=8,'chan'=4] {'chan'}, dimensions={0}, use_global_device_ids=true | all-gather | bytes 737280 | tf_op jit(solution)/shard_map/all_gather | solution.py:119
  49.6 7.6 %all_gather.7 = bf16[128,9,256]{2,0,1:T(8,128)(2,1)S(1)} all-gather(bf16[32,9,256]{2,0,1:T(8,128)(2,1)S(1)} %pad_maximum_fusion.1), channel_id=1, replica_groups=mesh['space'=8,'chan'=4] {'chan'}, dimensions={0}, use_global_device_ids=true | all-gather | bytes 737280 | tf_op jit(solution)/shard_map/all_gather | solution.py:138
  57.7 47.2 %while.29 = (s32[]{:T(128)}, f32[32,640]{1,0:T(8,128)S(1)}, f32[3,640]{1,0:T(4,128)S(1)}, f32[32,8]{0,1:T(8,128)S(1)}, s32[]{:T(128)}, /*index=5*/s32[8,2]{0,1:T...) while((s32[]{:T(128)}, f32[32,640]{1,0:T(8,128)S(1)}, ...), condition=%wide.region_19.22_spmd, body=%wide.region_5.21_spmd.sunk | while | flops 250567328 | bytes 19222200 | solution.py:183
  68.5 1.3 fusion.574
  71.6 1.0 fusion.580
  72.9 1.0 fusion.582
  75.4 1.0 fusion.586
  76.7 1.0 fusion.588
  77.9 1.0 fusion.590
  79.2 1.0 fusion.592
  91.7 1.3 fusion.574
  98.6 1.0 fusion.586
  99.9 1.0 fusion.588
  101.1 1.0 fusion.590
  102.4 1.0 fusion.592
  105.1 14.2 %psum.14 = f32[3,640]{0,1:T(8,128)S(1)} all-reduce(f32[3,640]{0,1:T(8,128)S(1)} %copy.73), channel_id=1, replica_groups=mesh['space'=8,'chan'=4] {'chan'}, use_global_device_ids=true, to_apply=%region_23.26 | all-reduce | flops 1920 | bytes 15360 | tf_op jit(solution)/shard_map/psum | solution.py:184
  119.3 195.9 %collective-permute-start.9 = (f32[3,128]{0,1:T(8,128)S(1)}, f32[3,128]{0,1:T(8,128)S(1)}, u32[]{:S(2)}, u32[]{:S(2)}) collective-permute-start(f32[3,128]{0,1:T(8,128)S(1)} %get-tuple-element.342), channel_id=1, source_target_pairs={{0,4},{4,0},{8,12},{12,8},{16,20},{20,16},{24,28},{28,24},{1,5},{5... | collective-permute-start | bytes 4616 | tf_op jit(solution)/shard_map/ppermute | solution.py:18
  315.3 2.9 collective-permute-start.7
  318.2 1.1 collective-permute-start.8
  319.3 2.0 collective-permute-start.10
  323.1 21.2 %psum.15 = f32[32,8]{0,1:T(8,128)} all-reduce(f32[32,8]{0,1:T(8,128)S(1)} %get-tuple-element.231), channel_id=1, replica_groups=mesh['space'=8,'chan'=4] {'space'}, use_global_device_ids=true, to_apply=%region_27.30 | all-reduce | flops 256 | bytes 2048 | tf_op jit(solution)/shard_map/psum | solution.py:197
  344.3 1.3 scatter_custom_fusion.3
  345.6 1.3 scatter_custom_fusion.4
  347.0 1.3 scatter_custom_fusion.5
  349.9 1.3 scatter_fusion
  351.2 1.3 scatter_fusion.1
  352.5 1.3 scatter_fusion.2
  (265 shorter events, 54.5 us)
Async XLA Ops:
  0.6 16.1 %copy-start = (bf16[3,128,128]{2,1,0:T(8,128)(2,1)S(1)}, bf16[3,128,128]{2,1,0:T(8,128)(2,1)}, u32[]{:S(2)}) copy-start(bf16[3,128,128]{2,1,0:T(8,128)(2,1)} %param.23) | copy-start | bytes 294916
  0.6 0.9 copy-start.10
  2.4 15.8 %collective-permute-start.2 = (bf16[32,128]{1,0:T(8,128)(2,1)S(1)}, bf16[32,128]{1,0:T(8,128)(2,1)S(1)}, u32[]{:S(2)}, u32[]{:S(2)}) collective-permute-start(bf16[32,128]{1,0:T(8,128)(2,1)S(1)} %bitcast_convert_fusion), channel_id=1, source_target_pairs={{0,16},{4,20},{8,24},{12,28},{16,0},{20,4},{24,8},{28,12},{1,17},{... | collective-permute-start | bytes 24584 | tf_op jit(solution)/shard_map/ppermute | solution.py:18
  7.3 1.7 copy-start.9
  7.3 10.9 %collective-permute-start.1 = (bf16[32,128]{1,0:T(8,128)(2,1)S(1)}, bf16[32,128]{1,0:T(8,128)(2,1)S(1)}, u32[]{:S(2)}, u32[]{:S(2)}) collective-permute-start(bf16[32,128]{1,0:T(8,128)(2,1)S(1)} %bitcast_convert_fusion.1), channel_id=1, source_target_pairs={{0,8},{4,12},{8,0},{12,4},{16,24},{20,28},{24,16},{28,20},{1,9},{5... | collective-permute-start | bytes 24584 | tf_op jit(solution)/shard_map/ppermute | solution.py:18
  9.8 7.5 %collective-permute-start.5 = (f32[3,128]{0,1:T(8,128)S(1)}, f32[3,128]{0,1:T(8,128)S(1)}, u32[]{:S(2)}, u32[]{:S(2)}) collective-permute-start(f32[3,128]{0,1:T(8,128)S(1)} %select_bitcast_fusion), channel_id=1, source_target_pairs={{0,16},{4,20},{8,24},{12,28},{16,0},{20,4},{24,8},{28,12},{1,17},{... | collective-permute-start | bytes 4616 | tf_op jit(solution)/shard_map/ppermute | solution.py:18
  11.0 7.0 %collective-permute-start.4 = (f32[3,128]{0,1:T(8,128)S(1)}, f32[3,128]{0,1:T(8,128)S(1)}, u32[]{:S(2)}, u32[]{:S(2)}) collective-permute-start(f32[3,128]{0,1:T(8,128)S(1)} %select_bitcast_fusion.1), channel_id=1, source_target_pairs={{0,8},{4,12},{8,0},{12,4},{16,24},{20,28},{24,16},{28,20},{1,9},{5... | collective-permute-start | bytes 4616 | tf_op jit(solution)/shard_map/ppermute | solution.py:18
  11.6 3.8 %copy-start.6 = (bf16[32,9,256]{2,0,1:T(8,128)(2,1)S(1)}, bf16[32,9,256]{2,0,1:T(8,128)(2,1)}, u32[]{:S(2)}) copy-start(bf16[32,9,256]{2,0,1:T(8,128)(2,1)} %param.24) | copy-start | bytes 442372
  12.4 5.7 %collective-permute-start.3 = (f32[3,128]{0,1:T(8,128)S(1)}, f32[3,128]{0,1:T(8,128)S(1)}, u32[]{:S(2)}, u32[]{:S(2)}) collective-permute-start(f32[3,128]{0,1:T(8,128)S(1)} %select_bitcast_fusion.2), channel_id=1, source_target_pairs={{0,4},{4,0},{8,12},{12,8},{16,20},{20,16},{24,28},{28,24},{1,5},{5... | collective-permute-start | bytes 4616 | tf_op jit(solution)/shard_map/ppermute | solution.py:18
  14.7 0.7 copy-start.11
  15.4 0.7 copy-start.12
  15.4 1.3 copy-start.1
  17.4 3.7 %collective-permute-start = (bf16[32,128]{1,0:T(8,128)(2,1)S(1)}, bf16[32,128]{1,0:T(8,128)(2,1)S(1)}, u32[]{:S(2)}, u32[]{:S(2)}) collective-permute-start(bf16[32,128]{1,0:T(8,128)(2,1)S(1)} %bitcast_convert_fusion.2), channel_id=1, source_target_pairs={{0,4},{4,0},{8,12},{12,8},{16,20},{20,16},{24,28},{28,24},{1,5},{5... | collective-permute-start | bytes 24584 | tf_op jit(solution)/shard_map/ppermute | solution.py:18
  18.2 2.9 copy-start.8
  21.1 0.7 copy-start.7
  41.1 0.6 copy-start.2
  64.9 0.8 copy-start.3
  88.1 0.8 copy-start.3
  119.3 203.1 %copy-start.5 = (f32[3,640]{0,1:T(8,128)}, f32[3,640]{0,1:T(8,128)S(1)}, u32[]{:S(2)}) copy-start(f32[3,640]{0,1:T(8,128)S(1)} %psum.14) | copy-start | bytes 23044
  119.3 202.0 %collective-permute-start.9 = (f32[3,128]{0,1:T(8,128)S(1)}, f32[3,128]{0,1:T(8,128)S(1)}, u32[]{:S(2)}, u32[]{:S(2)}) collective-permute-start(f32[3,128]{0,1:T(8,128)S(1)} %get-tuple-element.342), channel_id=1, source_target_pairs={{0,4},{4,0},{8,12},{12,8},{16,20},{20,16},{24,28},{28,24},{1,5},{5... | collective-permute-start | bytes 4616 | tf_op jit(solution)/shard_map/ppermute | solution.py:18
  315.2 33.8 %collective-permute-start.6 = (f32[32,128]{1,0:T(8,128)S(1)}, f32[32,128]{1,0:T(8,128)S(1)}, u32[]{:S(2)}, u32[]{:S(2)}) collective-permute-start(f32[32,128]{1,0:T(8,128)S(1)} %get-tuple-element.348), channel_id=1, source_target_pairs={{0,4},{4,0},{8,12},{12,8},{16,20},{20,16},{24,28},{28,24},{1,5},{5... | collective-permute-start | bytes 49160 | tf_op jit(solution)/shard_map/ppermute | solution.py:18
  315.3 33.8 %collective-permute-start.7 = (f32[32,128]{1,0:T(8,128)S(1)}, f32[32,128]{1,0:T(8,128)S(1)}, u32[]{:S(2)}, u32[]{:S(2)}) collective-permute-start(f32[32,128]{1,0:T(8,128)S(1)} %get-tuple-element.347), channel_id=1, source_target_pairs={{0,8},{4,12},{8,0},{12,4},{16,24},{20,28},{24,16},{28,20},{1,9},{5... | collective-permute-start | bytes 49160 | tf_op jit(solution)/shard_map/ppermute | solution.py:18
  318.2 31.0 %collective-permute-start.8 = (f32[32,128]{1,0:T(8,128)S(1)}, f32[32,128]{1,0:T(8,128)S(1)}, u32[]{:S(2)}, u32[]{:S(2)}) collective-permute-start(f32[32,128]{1,0:T(8,128)S(1)} %get-tuple-element.346), channel_id=1, source_target_pairs={{0,16},{4,20},{8,24},{12,28},{16,0},{20,4},{24,8},{28,12},{1,17},{... | collective-permute-start | bytes 49160 | tf_op jit(solution)/shard_map/ppermute | solution.py:18
  319.3 26.3 %collective-permute-start.10 = (f32[3,128]{0,1:T(8,128)S(1)}, f32[3,128]{0,1:T(8,128)S(1)}, u32[]{:S(2)}, u32[]{:S(2)}) collective-permute-start(f32[3,128]{0,1:T(8,128)S(1)} %get-tuple-element.341), channel_id=1, source_target_pairs={{0,8},{4,12},{8,0},{12,4},{16,24},{20,28},{24,16},{28,20},{1,9},{5... | collective-permute-start | bytes 4616 | tf_op jit(solution)/shard_map/ppermute | solution.py:18
  321.3 25.6 %collective-permute-start.11 = (f32[3,128]{0,1:T(8,128)S(1)}, f32[3,128]{0,1:T(8,128)S(1)}, u32[]{:S(2)}, u32[]{:S(2)}) collective-permute-start(f32[3,128]{0,1:T(8,128)S(1)} %get-tuple-element.340), channel_id=1, source_target_pairs={{0,16},{4,20},{8,24},{12,28},{16,0},{20,4},{24,8},{28,12},{1,17},{... | collective-permute-start | bytes 4616 | tf_op jit(solution)/shard_map/ppermute | solution.py:18
  322.4 0.7 copy-start.4
  322.4 21.9 %slice-start.1 = ((f32[3,640]{0,1:T(8,128)}), f32[3,256]{0,1:T(8,128)S(1)}, s32[]{:S(2)}) async-start(f32[3,640]{0,1:T(8,128)} %copy-done.5), calls=%async_computation.1 | async-start | bytes 262144 | tf_op jit(solution)/shard_map/slice | solution.py:186
  349.0 0.9 slice-start
where the time goes:
time: 359 us; the launch traced here: 355 us
  starting transfers between devices  211 us (59%)
  blocking collectives  50.5 us (14%)
  matrix products  43.7 us (12%)
  local copies, waits for them, and re-layouts  17.6 us (5%)
  loops' own time  15.4 us (4%)
  other arithmetic  12.2 us (3%)
    ppermute x12, starting transfers between devices, partner(): return lax.ppermute(value, axis, pairs)  211 us
    psum x1, blocking collectives, body(): grad_radial = lax.psum(grad_rad, 'space')  21.2 us
    dot_general x18, matrix products, backward_tile(): jnp.einsum('kij,cj->cki', pair_values, source_feat, preferred_element_typ...  17.3 us
    psum x1, blocking collectives, body(): dpos_src = lax.psum(dpos_src, 'chan')  14.2 us
    dot_general x18, matrix products, backward_tile(): jnp.einsum('cki,cj->kij', weighted, source_feat, preferred_element_type=j...  8.14 us
    another operation x1, loops' own time, body(): lax.fori_loop(0, live_count, backward_tile, init)  7.83 us
    all_gather x1, blocking collectives, body(): gathered_piece = lax.all_gather(dz_packed, 'chan', axis=0, tiled=True)  7.65 us
    another operation x1, loops' own time, body(): lax.fori_loop(0, live_count, forward_tile, jnp.zeros((chan_dev, component...  7.56 us
  transfers between devices with their start and end apart: 12, of which 1 were waited for; matrix products, arithmetic and copies ran while one was open for 3% of the time, Pallas kernels for 0%

commit v1 on v0

--- a/solution.py
+++ b/solution.py
@@ -194,7 +194,7 @@
         sent_rows = send_rows[level_bit]
         own_grad = own_grad.at[:, sent_rows].add(back_grad)
         own_dpos = own_dpos.at[:, sent_rows].add(back_pos)
-    grad_radial = lax.psum(grad_rad, "space")
+    grad_radial = jnp.sum(lax.all_gather(grad_rad, "space"), axis=0)
     return (result, own_grad.astype(jnp.bfloat16), -own_dpos, grad_radial)
 
 

time: 359 us -> 370 us (1.031)
  blocking collectives: 50.5 us -> 59.4 us
    all_gather x0 -> x1, blocking collectives: none -> 30.4 us  [body(): grad_radial = jnp.sum(lax.all_gather(grad_rad, 'space'), axis=0)]
    psum x1 -> x0, blocking collectives: 21.2 us -> none  [body(): grad_radial = lax.psum(grad_rad, 'space')]
  transfers between devices with their start and end apart: 12 -> 12, of which waited for: 1 -> 2; matrix products, arithmetic and copies ran while one was open for 3% -> 3% of each run, Pallas kernels for 0% -> 0%
where the time goes in v1:
time: 370 us; the launch traced here: 366 us
  starting transfers between devices  211 us (57%)
  blocking collectives  59.4 us (16%)
  matrix products  43.7 us (12%)
  local copies, waits for them, and re-layouts  17.6 us (5%)
  loops' own time  15.4 us (4%)
  other arithmetic  12.8 us (3%)
  waiting for transfers between devices  4.32 us (1%)
    ppermute x12, starting transfers between devices, partner(): return lax.ppermute(value, axis, pairs)  211 us
    all_gather x1, blocking collectives, body(): grad_radial = jnp.sum(lax.all_gather(grad_rad, 'space'), axis=0)  30.4 us
    dot_general x18, matrix products, backward_tile(): jnp.einsum('kij,cj->cki', pair_values, source_feat, preferred_element_typ...  17.3 us
    psum x1, blocking collectives, body(): dpos_src = lax.psum(dpos_src, 'chan')  13.9 us
    dot_general x18, matrix products, backward_tile(): jnp.einsum('cki,cj->kij', weighted, source_feat, preferred_element_type=j...  8.14 us
    another operation x1, loops' own time, body(): lax.fori_loop(0, live_count, backward_tile, init)  7.83 us
    all_gather x1, blocking collectives, body(): gathered_piece = lax.all_gather(dz_packed, 'chan', axis=0, tiled=True)  7.65 us
    another operation x1, loops' own time, body(): lax.fori_loop(0, live_count, forward_tile, jnp.zeros((chan_dev, component...  7.56 us
  transfers between devices with their start and end apart: 12, of which 2 were waited for; matrix products, arithmetic and copies ran while one was open for 3% of the time, Pallas kernels for 0%

profile of v1, /device:TPU:0, one launch (start us, length us, event | category | flops | bytes accessed | tf_op | source)
XLA Modules:
  0.0 365.8 jit_solution(13888910505952466924)
XLA Ops:
  2.4 4.1 %collective-permute-start.2 = (bf16[32,128]{1,0:T(8,128)(2,1)S(1)}, bf16[32,128]{1,0:T(8,128)(2,1)S(1)}, u32[]{:S(2)}, u32[]{:S(2)}) collective-permute-start(bf16[32,128]{1,0:T(8,128)(2,1)S(1)} %bitcast_convert_fusion), channel_id=1, source_target_pairs={{0,16},{4,20},{8,24},{12,28},{16,0},{20,4},{24,8},{28,12},{1,17},{... | collective-permute-start | bytes 24584 | tf_op jit(solution)/shard_map/ppermute | solution.py:18
  7.3 1.6 collective-permute-start.1
  12.4 1.6 collective-permute-start.3
  18.2 2.9 collective-permute-done
  21.8 19.3 %while.28 = (s32[]{:T(128)}, f32[32,9,256]{2,0,1:T(8,128)S(1)}, s32[]{:T(128)}, s32[8,2]{0,1:T(2,128)S(1)}, bf16[32,640]{1,0:T(8,128)(2,1)S(1)}, /*index=5*/f32[...) while((s32[]{:T(128)}, f32[32,9,256]{2,0,1:T(8,128)S(1)}, ...), condition=%wide.region_3.6_spmd, body=%wide.region_1.5_spmd.sunk | while | flops 83677216 | bytes 5811606 | solution.py:113
  41.7 7.5 %all_gather.12 = bf16[128,9,256]{2,0,1:T(8,128)(2,1)S(1)} all-gather(bf16[32,9,256]{2,0,1:T(8,128)(2,1)S(1)} %convert_element_type.217), channel_id=1, replica_groups=mesh['space'=8,'chan'=4] {'chan'}, dimensions={0}, use_global_device_ids=true | all-gather | bytes 737280 | tf_op jit(solution)/shard_map/all_gather | solution.py:119
  49.6 7.6 %all_gather.13 = bf16[128,9,256]{2,0,1:T(8,128)(2,1)S(1)} all-gather(bf16[32,9,256]{2,0,1:T(8,128)(2,1)S(1)} %pad_maximum_fusion.1), channel_id=1, replica_groups=mesh['space'=8,'chan'=4] {'chan'}, dimensions={0}, use_global_device_ids=true | all-gather | bytes 737280 | tf_op jit(solution)/shard_map/all_gather | solution.py:138
  57.7 47.2 %while.29 = (s32[]{:T(128)}, f32[32,640]{1,0:T(8,128)S(1)}, f32[3,640]{1,0:T(4,128)S(1)}, f32[32,8]{0,1:T(8,128)S(1)}, s32[]{:T(128)}, /*index=5*/s32[8,2]{0,1:T...) while((s32[]{:T(128)}, f32[32,640]{1,0:T(8,128)S(1)}, ...), condition=%wide.region_19.22_spmd, body=%wide.region_5.21_spmd.sunk | while | flops 250567328 | bytes 19222200 | solution.py:183
  68.5 1.3 fusion.574
  71.6 1.0 fusion.580
  75.4 1.0 fusion.586
  76.7 1.0 fusion.588
  77.9 1.0 fusion.590
  79.2 1.0 fusion.592
  91.7 1.3 fusion.574
  98.6 1.0 fusion.586
  99.9 1.0 fusion.588
  101.1 1.0 fusion.590
  102.4 1.0 fusion.592
  104.9 195.9 %collective-permute-start.6 = (f32[32,128]{1,0:T(8,128)S(1)}, f32[32,128]{1,0:T(8,128)S(1)}, u32[]{:S(2)}, u32[]{:S(2)}) collective-permute-start(f32[32,128]{1,0:T(8,128)S(1)} %get-tuple-element.352), channel_id=1, source_target_pairs={{0,4},{4,0},{8,12},{12,8},{16,20},{20,16},{24,28},{28,24},{1,5},{5... | collective-permute-start | bytes 49160 | tf_op jit(solution)/shard_map/ppermute | solution.py:18
  300.8 1.4 collective-permute-start.7
  302.2 2.5 collective-permute-start.8
  305.0 13.9 %psum.7 = f32[3,640]{0,1:T(8,128)S(1)} all-reduce(f32[3,640]{0,1:T(8,128)S(1)} %copy.94), channel_id=1, replica_groups=mesh['space'=8,'chan'=4] {'chan'}, use_global_device_ids=true, to_apply=%region_23.26 | all-reduce | flops 1920 | bytes 15360 | tf_op jit(solution)/shard_map/psum | solution.py:184
  319.4 1.6 collective-permute-start.10
  321.8 1.4 collective-permute-done.9
  323.6 30.4 %all-gather.1 = f32[8,32,8]{1,2,0:T(8,128)S(1)} all-gather(f32[1,32,8]{1,2,0:T(8,128)S(1)} %bitcast.689), channel_id=2, replica_groups=mesh['space'=8,'chan'=4] {'space'}, dimensions={0}, use_global_device_ids=true | all-gather | bytes 9216 | tf_op jit(solution)/shard_map/all_gather | solution.py:197
  355.5 1.3 scatter_custom_fusion.3
  356.8 1.3 scatter_custom_fusion.4
  358.2 1.3 scatter_custom_fusion.5
  361.1 1.3 scatter_fusion
  362.4 1.3 scatter_fusion.1
  363.7 1.3 scatter_fusion.2
  (266 shorter events, 56.9 us)
Async XLA Ops:
  0.6 16.1 %copy-start = (bf16[3,128,128]{2,1,0:T(8,128)(2,1)S(1)}, bf16[3,128,128]{2,1,0:T(8,128)(2,1)}, u32[]{:S(2)}) copy-start(bf16[3,128,128]{2,1,0:T(8,128)(2,1)} %param.23) | copy-start | bytes 294916
  0.6 0.9 copy-start.10
  2.4 15.8 %collective-permute-start.2 = (bf16[32,128]{1,0:T(8,128)(2,1)S(1)}, bf16[32,128]{1,0:T(8,128)(2,1)S(1)}, u32[]{:S(2)}, u32[]{:S(2)}) collective-permute-start(bf16[32,128]{1,0:T(8,128)(2,1)S(1)} %bitcast_convert_fusion), channel_id=1, source_target_pairs={{0,16},{4,20},{8,24},{12,28},{16,0},{20,4},{24,8},{28,12},{1,17},{... | collective-permute-start | bytes 24584 | tf_op jit(solution)/shard_map/ppermute | solution.py:18
  7.3 1.7 copy-start.9
  7.3 10.9 %collective-permute-start.1 = (bf16[32,128]{1,0:T(8,128)(2,1)S(1)}, bf16[32,128]{1,0:T(8,128)(2,1)S(1)}, u32[]{:S(2)}, u32[]{:S(2)}) collective-permute-start(bf16[32,128]{1,0:T(8,128)(2,1)S(1)} %bitcast_convert_fusion.1), channel_id=1, source_target_pairs={{0,8},{4,12},{8,0},{12,4},{16,24},{20,28},{24,16},{28,20},{1,9},{5... | collective-permute-start | bytes 24584 | tf_op jit(solution)/shard_map/ppermute | solution.py:18
  9.8 7.5 %collective-permute-start.5 = (f32[3,128]{0,1:T(8,128)S(1)}, f32[3,128]{0,1:T(8,128)S(1)}, u32[]{:S(2)}, u32[]{:S(2)}) collective-permute-start(f32[3,128]{0,1:T(8,128)S(1)} %select_bitcast_fusion), channel_id=1, source_target_pairs={{0,16},{4,20},{8,24},{12,28},{16,0},{20,4},{24,8},{28,12},{1,17},{... | collective-permute-start | bytes 4616 | tf_op jit(solution)/shard_map/ppermute | solution.py:18
  11.0 7.0 %collective-permute-start.4 = (f32[3,128]{0,1:T(8,128)S(1)}, f32[3,128]{0,1:T(8,128)S(1)}, u32[]{:S(2)}, u32[]{:S(2)}) collective-permute-start(f32[3,128]{0,1:T(8,128)S(1)} %select_bitcast_fusion.1), channel_id=1, source_target_pairs={{0,8},{4,12},{8,0},{12,4},{16,24},{20,28},{24,16},{28,20},{1,9},{5... | collective-permute-start | bytes 4616 | tf_op jit(solution)/shard_map/ppermute | solution.py:18
  11.6 3.8 %copy-start.6 = (bf16[32,9,256]{2,0,1:T(8,128)(2,1)S(1)}, bf16[32,9,256]{2,0,1:T(8,128)(2,1)}, u32[]{:S(2)}) copy-start(bf16[32,9,256]{2,0,1:T(8,128)(2,1)} %param.24) | copy-start | bytes 442372
  12.4 5.7 %collective-permute-start.3 = (f32[3,128]{0,1:T(8,128)S(1)}, f32[3,128]{0,1:T(8,128)S(1)}, u32[]{:S(2)}, u32[]{:S(2)}) collective-permute-start(f32[3,128]{0,1:T(8,128)S(1)} %select_bitcast_fusion.2), channel_id=1, source_target_pairs={{0,4},{4,0},{8,12},{12,8},{16,20},{20,16},{24,28},{28,24},{1,5},{5... | collective-permute-start | bytes 4616 | tf_op jit(solution)/shard_map/ppermute | solution.py:18
  14.7 0.7 copy-start.11
  15.4 0.7 copy-start.12
  15.4 1.3 copy-start.1
  17.4 3.7 %collective-permute-start = (bf16[32,128]{1,0:T(8,128)(2,1)S(1)}, bf16[32,128]{1,0:T(8,128)(2,1)S(1)}, u32[]{:S(2)}, u32[]{:S(2)}) collective-permute-start(bf16[32,128]{1,0:T(8,128)(2,1)S(1)} %bitcast_convert_fusion.2), channel_id=1, source_target_pairs={{0,4},{4,0},{8,12},{12,8},{16,20},{20,16},{24,28},{28,24},{1,5},{5... | collective-permute-start | bytes 24584 | tf_op jit(solution)/shard_map/ppermute | solution.py:18
  18.2 2.9 copy-start.8
  21.1 0.7 copy-start.7
  41.1 0.6 copy-start.2
  64.9 0.8 copy-start.3
  88.1 0.8 copy-start.3
  104.9 255.2 %collective-permute-start.6 = (f32[32,128]{1,0:T(8,128)S(1)}, f32[32,128]{1,0:T(8,128)S(1)}, u32[]{:S(2)}, u32[]{:S(2)}) collective-permute-start(f32[32,128]{1,0:T(8,128)S(1)} %get-tuple-element.352), channel_id=1, source_target_pairs={{0,4},{4,0},{8,12},{12,8},{16,20},{20,16},{24,28},{28,24},{1,5},{5... | collective-permute-start | bytes 49160 | tf_op jit(solution)/shard_map/ppermute | solution.py:18
  300.8 59.5 %collective-permute-start.7 = (f32[32,128]{1,0:T(8,128)S(1)}, f32[32,128]{1,0:T(8,128)S(1)}, u32[]{:S(2)}, u32[]{:S(2)}) collective-permute-start(f32[32,128]{1,0:T(8,128)S(1)} %get-tuple-element.351), channel_id=1, source_target_pairs={{0,8},{4,12},{8,0},{12,4},{16,24},{20,28},{24,16},{28,20},{1,9},{5... | collective-permute-start | bytes 49160 | tf_op jit(solution)/shard_map/ppermute | solution.py:18
  302.2 58.2 %collective-permute-start.8 = (f32[32,128]{1,0:T(8,128)S(1)}, f32[32,128]{1,0:T(8,128)S(1)}, u32[]{:S(2)}, u32[]{:S(2)}) collective-permute-start(f32[32,128]{1,0:T(8,128)S(1)} %get-tuple-element.350), channel_id=1, source_target_pairs={{0,16},{4,20},{8,24},{12,28},{16,0},{20,4},{24,8},{28,12},{1,17},{... | collective-permute-start | bytes 49160 | tf_op jit(solution)/shard_map/ppermute | solution.py:18
  318.8 35.3 %copy-start.5 = (f32[3,640]{0,1:T(8,128)}, f32[3,640]{0,1:T(8,128)S(1)}, u32[]{:S(2)}) copy-start(f32[3,640]{0,1:T(8,128)S(1)} %psum.7) | copy-start | bytes 23044
  318.9 4.3 %collective-permute-start.9 = (f32[3,128]{0,1:T(8,128)S(1)}, f32[3,128]{0,1:T(8,128)S(1)}, u32[]{:S(2)}, u32[]{:S(2)}) collective-permute-start(f32[3,128]{0,1:T(8,128)S(1)} %get-tuple-element.346), channel_id=1, source_target_pairs={{0,4},{4,0},{8,12},{12,8},{16,20},{20,16},{24,28},{28,24},{1,5},{5... | collective-permute-start | bytes 4616 | tf_op jit(solution)/shard_map/ppermute | solution.py:18
  319.4 37.4 %collective-permute-start.10 = (f32[3,128]{0,1:T(8,128)S(1)}, f32[3,128]{0,1:T(8,128)S(1)}, u32[]{:S(2)}, u32[]{:S(2)}) collective-permute-start(f32[3,128]{0,1:T(8,128)S(1)} %get-tuple-element.345), channel_id=1, source_target_pairs={{0,8},{4,12},{8,0},{12,4},{16,24},{20,28},{24,16},{28,20},{1,9},{5... | collective-permute-start | bytes 4616 | tf_op jit(solution)/shard_map/ppermute | solution.py:18
  323.2 34.9 %collective-permute-start.11 = (f32[3,128]{0,1:T(8,128)S(1)}, f32[3,128]{0,1:T(8,128)S(1)}, u32[]{:S(2)}, u32[]{:S(2)}) collective-permute-start(f32[3,128]{0,1:T(8,128)S(1)} %get-tuple-element.344), channel_id=1, source_target_pairs={{0,16},{4,20},{8,24},{12,28},{16,0},{20,4},{24,8},{28,12},{1,17},{... | collective-permute-start | bytes 4616 | tf_op jit(solution)/shard_map/ppermute | solution.py:18
  354.2 0.7 copy-start.4
  354.2 1.3 slice-start.1
  360.2 0.9 slice-start
